TPU v7x, 256 devices: a whole 4x4x8 slice. The times are simulated.
256 devices in a mesh: seq: 32 (over x, y, core), exp: 8 (over z).
Axes of the slice: x: 4, y: 4, z: 8, core: 2. Of those that a mesh axis runs over, the one named last changes fastest.
Arguments:
- query_rows: bfloat16 [2048, 8192], P('seq', 'exp'), may hold values from -6 to 6
- key_rows: bfloat16 [2048, 8192], P('seq', 'exp'), may hold values from -6 to 6
- value_rows: bfloat16 [2048, 8192], P('seq', 'exp'), may hold values from -120 to 120
- log_decay: float32 [2048, 64], P('seq', 'exp'), may hold values from -1.4625 to 0, as said below
- out_weight: bfloat16 [8192, 6144], P('exp', 'seq'), may hold values from -0.0625 to 0.0625
- residual: bfloat16 [2048, 6144], P('exp', 'seq'), may hold values from -18 to 18
- routes: int32 [2048, 2], P('exp'), may hold values from 0 to 7, all different within a row; in each aligned block of 256 rows (0 to 255, 256 to 511, ...) at most 128 rows name the same one
- gate_weight: bfloat16 [8, 9216, 6144], P('exp', 'seq'), may hold values from -0.078125 to 0.078125
- up_weight: bfloat16 [8, 9216, 6144], P('exp', 'seq'), may hold values from -0.078125 to 0.078125
Outputs:
- residual_out: bfloat16 [2048, 6144], P('exp', 'seq')
- expert_hidden: bfloat16 [8, 9216, 1024], P('exp', 'seq')
Inputs may be any that keep to these rules, and one draw needn't show every extreme that they name: `routes`: each token names 2 different experts; within one source group of 256 tokens no expert is named more than 128 times. `log_decay`: every entry is negative.
All inputs are finite; a program needn't handle non-finite values.
Results may differ from a plain program's by a relative error of at most 0.0065.
Values may be sent and summed in bfloat16 or wider, within the bound.
No kernel may reach another device: no remote copies, remote signals or barrier semaphores. Data moves between devices by JAX's collectives and lax.ppermute only.
A program may use at most 128 MiB of HBM per device.

v0:
```python
import jax
import jax.numpy as jnp
from jax import lax
from jax.sharding import Mesh
from jax.sharding import PartitionSpec as P

D = 6144
HEAD_DIM = 128
SEQ = ("seq_0", "seq_1", "seq_2")
precise = lax.Precision.HIGHEST
contract_last = (((1,), (1,)), ((), ()))


def nothing_yet(shard, identity):
    return jax.tree.map(
        lambda a, e: jnp.broadcast_to(jnp.asarray(e, a.dtype), a.shape), shard, identity
    )


def carried_in(shard, axes, combine, identity):
    before = start = nothing_yet(shard, identity)
    so_far = shard
    for axis in reversed(axes):
        peers, place = (lax.axis_size(axis), lax.axis_index(axis))
        pieces = jax.tree.map(lambda part: lax.all_gather(part, axis), so_far)
        inside, so_far = (start, start)
        for k in range(peers):
            passed = k < place
            so_far = combine(so_far, jax.tree.map(lambda part: part[k], pieces))
            inside = jax.tree.map(lambda new, old: jnp.where(passed, new, old), so_far, inside)
        before = combine(inside, before)
    return before


def link_states(earlier, later):
    return (earlier[0] * later[0], later[0][:, None, None] * earlier[1] + later[1])


def swap_cores(tree):
    return jax.tree.map(lambda part: lax.ppermute(part, "seq_2", [(0, 1), (1, 0)]), tree)


def prefix_over(own, axis):
    peers, place = (lax.axis_size(axis), lax.axis_index(axis))
    shifted = [own] + [
        jax.tree.map(
            lambda part: lax.ppermute(part, axis, [(i, (i + d) % peers) for i in range(peers)]), own
        )
        for d in range(1, peers)
    ]
    start = nothing_yet(own, (1.0, 0.0))
    before, total = (start, start)
    for k in range(peers):
        lag = (place - k) % peers
        piece = jax.tree.map(
            lambda *opts: jnp.select([lag == d for d in range(peers)], opts), *shifted
        )
        total = link_states(total, piece)
        passed = k < place
        before = jax.tree.map(lambda new, old: jnp.where(passed, new, old), total, before)
    return (before, total)


def entering_state(decay, state):
    core = lax.axis_index("seq_2")
    other = swap_cores((decay, state))
    first = jax.tree.map(
        lambda mine, theirs: jnp.where(core == 0, mine, theirs), (decay, state), other
    )
    second = jax.tree.map(
        lambda mine, theirs: jnp.where(core == 0, theirs, mine), (decay, state), other
    )
    chip = link_states(first, second)
    half = decay.shape[0] // 2
    mine = jax.tree.map(lambda part: lax.dynamic_slice_in_dim(part, core * half, half, 0), chip)
    along_y, row = prefix_over(mine, "seq_1")
    along_x, _ = prefix_over(row, "seq_0")
    chip_before = link_states(along_x, along_y)
    theirs = swap_cores(chip_before)
    whole = jax.tree.map(
        lambda a, b: jnp.where(core == 0, jnp.concatenate([a, b], 0), jnp.concatenate([b, a], 0)),
        chip_before,
        theirs,
    )
    return jnp.where(core == 0, whole[1], first[0][:, None, None] * whole[1] + first[1])


def finish_rows(gate_sum, up_sum, squares):
    inv_rms = lax.rsqrt(squares / D + 1e-06)[None, :]
    return (jax.nn.silu(gate_sum * inv_rms) * (up_sum * inv_rms)).astype(jnp.bfloat16)


def body(
    query_rows,
    key_rows,
    value_rows,
    log_decay,
    out_weight,
    residual,
    routes,
    gate_weight,
    up_weight,
):
    positions, head_cols = query_rows.shape
    heads_here = head_cols // HEAD_DIM
    queries = query_rows.astype(jnp.float32).reshape(positions, heads_here, HEAD_DIM)
    keys_here = key_rows.astype(jnp.float32).reshape(positions, heads_here, HEAD_DIM)
    values_here = value_rows.astype(jnp.float32).reshape(positions, heads_here, HEAD_DIM)
    cumulative = jnp.cumsum(log_decay, axis=0)
    closing = cumulative[-1]
    key_scaled = keys_here * jnp.exp(closing[None, :] - cumulative)[:, :, None]
    local_state = jnp.einsum("shd,she->hde", key_scaled, values_here, precision=precise)
    entering = entering_state(jnp.exp(closing), local_state)
    later = lax.broadcasted_iota(jnp.int32, (positions, positions), 0)
    earlier = lax.broadcasted_iota(jnp.int32, (positions, positions), 1)
    causal = (later >= earlier)[None]
    carried = jnp.einsum(
        "thd,hde->the", queries * jnp.exp(cumulative)[:, :, None], entering, precision=precise
    )
    scores = jnp.einsum("thd,shd->hts", queries, keys_here, precision=precise)
    spread = cumulative.T[:, :, None] - cumulative.T[:, None, :]
    weights = jnp.where(causal, jnp.exp(jnp.where(causal, spread, 0.0)), 0.0)
    within = jnp.einsum("hts,she->the", scores * weights, values_here, precision=precise)
    head_raw = carried + within
    normed = head_raw * lax.rsqrt(jnp.mean(head_raw * head_raw, axis=-1, keepdims=True) + 1e-06)
    normed = normed.astype(jnp.bfloat16).reshape(positions, head_cols)
    gathered = lax.all_gather(normed, SEQ, axis=0, tiled=True)
    row_block = gathered
    attended = lax.psum_scatter(
        jnp.dot(row_block, out_weight, preferred_element_type=jnp.float32),
        "exp",
        scatter_dimension=0,
        tiled=True,
    )
    residual_out = (residual.astype(jnp.float32) + attended).astype(jnp.bfloat16)
    group_rows = routes.shape[0]
    choices_each = routes.shape[1]
    experts = lax.axis_size("exp")
    capacity = 4 * group_rows // experts
    route_flat = routes.reshape(-1)
    expert_ids = lax.broadcasted_iota(jnp.int32, (1, experts), 1)
    onehot = (route_flat[:, None] == expert_ids).astype(jnp.int32)
    slot_index = jnp.sum(jnp.cumsum(onehot, axis=0) * onehot, axis=1) - 1
    target = route_flat * capacity + slot_index
    w_gate = gate_weight[0]
    w_up = up_weight[0]
    hidden_rows = w_gate.shape[0]
    columns = residual_out.shape[1]
    buffer = jnp.zeros((experts * capacity, columns), jnp.bfloat16)
    buffer = buffer.at[target].set(jnp.repeat(residual_out, choices_each, axis=0))
    received = lax.all_to_all(
        buffer.reshape(experts, capacity, columns), "exp", split_axis=0, concat_axis=0, tiled=True
    )
    sources, entries, gathered_columns = received.shape
    slices = received.reshape(sources * entries, gathered_columns)
    row_block = lax.all_gather(slices, SEQ, axis=1, tiled=True)
    squares = jnp.einsum("rd,rd->r", row_block, row_block, preferred_element_type=jnp.float32)
    gate_sum = lax.dot_general(w_gate, row_block, contract_last, preferred_element_type=jnp.float32)
    up_sum = lax.dot_general(w_up, row_block, contract_last, preferred_element_type=jnp.float32)
    expert_hidden = finish_rows(gate_sum, up_sum, squares).reshape(hidden_rows, sources, entries)
    return (residual_out, expert_hidden.reshape(1, hidden_rows, experts * capacity))


def solution(mesh):
    torus = Mesh(
        mesh.devices.reshape(4, 4, 2, mesh.shape["exp"]), ("seq_0", "seq_1", "seq_2", "exp")
    )
    in_specs = (
        P(SEQ, "exp"),
        P(SEQ, "exp"),
        P(SEQ, "exp"),
        P(SEQ, "exp"),
        P("exp", SEQ),
        P("exp", SEQ),
        P("exp", None),
        P("exp", SEQ, None),
        P("exp", SEQ, None),
    )
    out_specs = (P("exp", SEQ), P("exp", SEQ, None))
    return jax.shard_map(body, mesh=torus, in_specs=in_specs, out_specs=out_specs, check_vma=False)
```

profile of v0, /device:TPU:1, one launch (start us, length us, event | category | flops | bytes accessed | tf_op | source)
XLA Modules:
  0.0 311.5 jit_solution(16042389560862939219)
XLA Ops:
  7.2 1.5 copy.69
  8.8 1.4 reduce_window_sum.26
  10.9 3.2 %collective-permute-start = (f32[8]{0:T(128)S(1)}, f32[8]{0:T(128)S(1)}, u32[]{:S(2)}, u32[]{:S(2)}) collective-permute-start(f32[8]{0:T(128)S(1)} %fusion.59), channel_id=1, source_target_pairs={{0,8},{8,0},{1,9},{9,1},{2,10},{10,2},{3,11},{11,3},{4,12},{12,4},... | collective-permute-start | bytes 104 | tf_op jit(solution)/shard_map/ppermute | solution.py:40
  14.8 1.4 fusion.61
  17.0 2.4 fusion.36
  49.0 2.3 collective-permute-start.3
  55.4 2.5 collective-permute-start.6
  58.5 1.9 collective-permute-done.10
  62.0 7.3 %collective-permute-done.8 = f32[4,128,128]{2,1,0:T(8,128)S(1)} collective-permute-done((f32[4,128,128]{2,1,0:T(8,128)S(1)}, f32[4,128,128]{2,1,0:T(8,128)S(1)}, u32[]{:S(2)}, u32[]{:S(2)}) %collective-permute-start.8) | collective-permute-done | bytes 262176 | tf_op jit(solution)/shard_map/ppermute | solution.py:47
  69.6 2.8 collective-permute-start.12
  72.8 2.4 collective-permute-start.13
  75.2 3.5 %collective-permute-done.12 = f32[4,128,128]{2,1,0:T(8,128)S(1)} collective-permute-done((f32[4,128,128]{2,1,0:T(8,128)S(1)}, f32[4,128,128]{2,1,0:T(8,128)S(1)}, u32[]{:S(2)}, u32[]{:S(2)}) %collective-permute-start.12) | collective-permute-done | bytes 262176 | tf_op jit(solution)/shard_map/ppermute | solution.py:47
  78.6 6.4 %collective-permute-done.11 = f32[4,128,128]{2,1,0:T(8,128)S(1)} collective-permute-done((f32[4,128,128]{2,1,0:T(8,128)S(1)}, f32[4,128,128]{2,1,0:T(8,128)S(1)}, u32[]{:S(2)}, u32[]{:S(2)}) %collective-permute-start.11) | collective-permute-done | bytes 262176 | tf_op jit(solution)/shard_map/ppermute | solution.py:47
  85.0 1.4 select_add_fusion
  90.1 2.2 multiply_reduce_fusion
  93.2 51.6 %all-gather.3.cloned.1.call-done = bf16[2048,1024]{1,0:T(8,128)(2,1)} async-done(((bf16[64,1024]{1,0:T(8,128)(2,1)}), bf16[2048,1024]{1,0:T(8,128)(2,1)}) %all-gather.3.cloned.1.call-update) | async-done | bytes 4194320 | tf_op jit(solution)/shard_map/all_gather | solution.py:127
  144.8 5.0 %fusion.62 = f32[2048,192]{0,1:T(8,128)} fusion(bf16[2048,1024]{1,0:T(8,128)(2,1)} %all-gather.3.cloned.1.call-done, bf16[1024,192]{0,1:T(8,128)(2,1)} %param.13), kind=kOutput, calls=%fused_computation.128 | convolution fusion | flops 805306368 | bytes 6160384 | tf_op jit(solution)/shard_map/dot_general | solution.py:130
  151.7 1.6 eq.212
  154.1 1.6 mul.219
  156.3 2.2 reduce-window.6
  162.8 22.7 %reduce-scatter.2.cloned.1.call-done = f32[256,192]{0,1:T(8,128)} async-done(((f32[2048,192]{0,1:T(8,128)}), f32[256,192]{0,1:T(8,128)}) %reduce-scatter.2.cloned.1.call-update) | async-done | bytes 196624 | tf_op jit(solution)/shard_map/reduce_scatter | solution.py:129
  185.4 1.6 add_convert_fusion
  187.1 1.6 copy.84
  188.7 1.7 broadcast_in_dim.122
  190.5 1.9 reshape.145
  192.3 3.5 %scatter_custom_fusion = bf16[1024,192]{1,0:T(8,128)(2,1)} fusion(s32[512]{0:T(512)S(1)} %bitcast.151, bf16[512,192]{1,0:T(8,128)(2,1)} %reshape.145, bf16[]{:T(256)} %constant.147.clone.1), kind=kCustom, calls=%fused_computation.26 | custom fusion | bytes 393728 | tf_op jit(solution)/shard_map/scatter | solution.py:150
  195.9 2.0 copy.86
  197.9 15.8 %all_to_all.5 = bf16[8,128,192]{1,2,0:T(8,128)(2,1)S(1)} all-to-all(bf16[8,128,192]{1,2,0:T(8,128)(2,1)} %copy.86), channel_id=1, replica_groups=mesh['seq_0'=4,'seq_1'=4,'seq_2'=2,'exp'=8] {'exp'}, dimensions={0} | all-to-all | bytes 786432 | tf_op jit(solution)/shard_map/all_to_all | solution.py:151
  214.5 69.3 %all-gather.5.cloned.1.call-done = bf16[1024,6144]{0,1:T(8,128)(2,1)} async-done(((bf16[1024,192]{0,1:T(8,128)(2,1)}), bf16[1024,6144]{0,1:T(8,128)(2,1)}) %all-gather.5.cloned.1.call-update) | async-done | bytes 12582928 | tf_op jit(solution)/shard_map/all_gather | solution.py:156
  283.8 7.1 %fusion = f32[1024]{0:T(1024)S(1)} fusion(bf16[1024,6144]{0,1:T(8,128)(2,1)} %all-gather.5.cloned.1.call-done), kind=kLoop, calls=%fused_computation.2 | loop fusion | flops 18873344 | bytes 12587008 | tf_op jit(solution)/shard_map/rd,rd->r/dot_general | solution.py:157
  290.9 7.0 %fusion.17 = f32[288,1024]{1,0:T(8,128)S(1)} fusion(bf16[1024,6144]{0,1:T(8,128)(2,1)} %all-gather.5.cloned.1.call-done, bf16[1,288,6144]{2,1,0:T(8,128)(2,1)S(1)} %copy-done, f32[1024]{0:T(1024)S(1)} %add_rsqrt_fusion), kind=kOutput, calls=%fused_computation.11 | convolution fusion | flops 3624173568 | bytes 17305600 | tf_op jit(solution)/shard_map/dot_general | solution.py:158
  300.1 4.9 %fusion.23 = bf16[1,288,1024]{2,1,0:T(8,128)(2,1)} fusion(bf16[1024,6144]{0,1:T(8,128)(2,1)S(1)} %copy-done.1, bf16[1,288,6144]{2,1,0:T(8,128)(2,1)S(1)} %copy-done.5, f32[288,1024]{1,0:T(8,128)S(1)} %fusion.17, f32[1024]{0:T(1024)S(1)} %add_rsqrt_fusion), kind=kOutput, calls=%fused_computation.13 | convolution fusion | flops 3625943040 | bytes 17895424 | tf_op jit(solution)/shard_map/dot_general | solution.py:159
  (90 shorter events, 33.9 us)
Async XLA Ops:
  7.2 283.7 %copy-start = (bf16[1,288,6144]{2,1,0:T(8,128)(2,1)S(1)}, bf16[1,288,6144]{2,1,0:T(8,128)(2,1)}, u32[]{:S(2)}) copy-start(bf16[1,288,6144]{2,1,0:T(8,128)(2,1)} %param.16) | copy-start | bytes 10616836
  7.2 137.6 %all-gather.3.cloned.1.call-start = ((), (), s32[]{:S(2)}) async-start(), calls=%async_computation.2 | async-start | bytes 4325376 | tf_op jit(solution)/shard_map/all_gather | solution.py:127
  10.9 35.7 %collective-permute-start = (f32[8]{0:T(128)S(1)}, f32[8]{0:T(128)S(1)}, u32[]{:S(2)}, u32[]{:S(2)}) collective-permute-start(f32[8]{0:T(128)S(1)} %fusion.59), channel_id=1, source_target_pairs={{0,8},{8,0},{1,9},{9,1},{2,10},{10,2},{3,11},{11,3},{4,12},{12,4},... | collective-permute-start | bytes 104 | tf_op jit(solution)/shard_map/ppermute | solution.py:40
  19.5 31.9 %collective-permute-start.7 = (f32[8,128,128]{2,1,0:T(8,128)}, f32[8,128,128]{2,1,0:T(8,128)}, u32[]{:S(2)}, u32[]{:S(2)}) collective-permute-start(f32[8,128,128]{2,1,0:T(8,128)} %fusion.36), channel_id=1, source_target_pairs={{0,8},{8,0},{1,9},{9,1},{2,10},{10,2},{3,11},{11,3},{4,12},{12,4},... | collective-permute-start | bytes 1572872 | tf_op jit(solution)/shard_map/ppermute | solution.py:40
  46.6 40.5 %copy-start.3 = (bf16[64,1024]{1,0:T(8,128)(2,1)S(1)}, bf16[64,1024]{1,0:T(8,128)(2,1)}, u32[]{:S(2)}) copy-start(bf16[64,1024]{1,0:T(8,128)(2,1)} %param.10) | copy-start | bytes 393220
  46.6 40.5 %copy-start.6 = (bf16[64,1024]{1,0:T(8,128)(2,1)S(1)}, bf16[64,1024]{1,0:T(8,128)(2,1)}, u32[]{:S(2)}) copy-start(bf16[64,1024]{1,0:T(8,128)(2,1)} %param.9) | copy-start | bytes 393220
  47.4 7.4 %collective-permute-start.2 = (f32[4]{0:T(128)S(1)}, f32[4]{0:T(128)S(1)}, u32[]{:S(2)}, u32[]{:S(2)}) collective-permute-start(f32[4]{0:T(128)S(1)} %dynamic_slice.6), channel_id=1, source_target_pairs={{0,32},{16,48},{32,0},{48,16},{1,33},{17,49},{33,1},{49,17},{2,34}... | collective-permute-start | bytes 56 | tf_op jit(solution)/shard_map/ppermute | solution.py:47
  48.6 6.7 %collective-permute-start.1 = (f32[4]{0:T(128)S(1)}, f32[4]{0:T(128)S(1)}, u32[]{:S(2)}, u32[]{:S(2)}) collective-permute-start(f32[4]{0:T(128)S(1)} %dynamic_slice.6), channel_id=1, source_target_pairs={{0,16},{16,32},{32,48},{48,0},{1,17},{17,33},{33,49},{49,1},{2,18}... | collective-permute-start | bytes 56 | tf_op jit(solution)/shard_map/ppermute | solution.py:47
  49.0 6.3 %collective-permute-start.3 = (f32[4]{0:T(128)S(1)}, f32[4]{0:T(128)S(1)}, u32[]{:S(2)}, u32[]{:S(2)}) collective-permute-start(f32[4]{0:T(128)S(1)} %dynamic_slice.6), channel_id=1, source_target_pairs={{0,48},{16,0},{32,16},{48,32},{1,49},{17,1},{33,17},{49,33},{2,50}... | collective-permute-start | bytes 56 | tf_op jit(solution)/shard_map/ppermute | solution.py:47
  52.5 16.9 %copy-start.2 = (f32[8,128,128]{2,1,0:T(8,128)}, f32[8,128,128]{2,1,0:T(8,128)S(1)}, u32[]{:S(2)}) copy-start(f32[8,128,128]{2,1,0:T(8,128)S(1)} %broadcast_select_fusion) | copy-start | bytes 1572868
  53.8 6.5 %collective-permute-start.10 = (f32[4,128,128]{2,1,0:T(8,128)S(1)}, f32[4,128,128]{2,1,0:T(8,128)S(1)}, u32[]{:S(2)}, u32[]{:S(2)}) collective-permute-start(f32[4,128,128]{2,1,0:T(8,128)S(1)} %fusion.30), channel_id=1, source_target_pairs={{0,48},{16,0},{32,16},{48,32},{1,49},{17,1},{33,17},{49,33},{2,50}... | collective-permute-start | bytes 786440 | tf_op jit(solution)/shard_map/ppermute | solution.py:47
  53.9 8.1 %collective-permute-start.9 = (f32[4,128,128]{2,1,0:T(8,128)S(1)}, f32[4,128,128]{2,1,0:T(8,128)S(1)}, u32[]{:S(2)}, u32[]{:S(2)}) collective-permute-start(f32[4,128,128]{2,1,0:T(8,128)S(1)} %fusion.30), channel_id=1, source_target_pairs={{0,32},{16,48},{32,0},{48,16},{1,33},{17,49},{33,1},{49,17},{2,34}... | collective-permute-start | bytes 786440 | tf_op jit(solution)/shard_map/ppermute | solution.py:47
  54.9 14.5 %collective-permute-start.8 = (f32[4,128,128]{2,1,0:T(8,128)S(1)}, f32[4,128,128]{2,1,0:T(8,128)S(1)}, u32[]{:S(2)}, u32[]{:S(2)}) collective-permute-start(f32[4,128,128]{2,1,0:T(8,128)S(1)} %fusion.30), channel_id=1, source_target_pairs={{0,16},{16,32},{32,48},{48,0},{1,17},{17,33},{33,49},{49,1},{2,18}... | collective-permute-start | bytes 786440 | tf_op jit(solution)/shard_map/ppermute | solution.py:47
  55.4 17.3 %collective-permute-start.6 = (f32[4]{0:T(128)S(1)}, f32[4]{0:T(128)S(1)}, u32[]{:S(2)}, u32[]{:S(2)}) collective-permute-start(f32[4]{0:T(128)S(1)} %get-tuple-element.19), channel_id=1, source_target_pairs={{0,192},{64,0},{128,64},{192,128},{1,193},{65,1},{129,65},{193,129... | collective-permute-start | bytes 56 | tf_op jit(solution)/shard_map/ppermute | solution.py:47
  57.9 17.2 %collective-permute-start.5 = (f32[4]{0:T(128)S(1)}, f32[4]{0:T(128)S(1)}, u32[]{:S(2)}, u32[]{:S(2)}) collective-permute-start(f32[4]{0:T(128)S(1)} %get-tuple-element.19), channel_id=1, source_target_pairs={{0,128},{64,192},{128,0},{192,64},{1,129},{65,193},{129,1},{193,65... | collective-permute-start | bytes 56 | tf_op jit(solution)/shard_map/ppermute | solution.py:47
  60.3 14.8 %collective-permute-start.4 = (f32[4]{0:T(128)S(1)}, f32[4]{0:T(128)S(1)}, u32[]{:S(2)}, u32[]{:S(2)}) collective-permute-start(f32[4]{0:T(128)S(1)} %get-tuple-element.19), channel_id=1, source_target_pairs={{0,64},{64,128},{128,192},{192,0},{1,65},{65,129},{129,193},{193,1... | collective-permute-start | bytes 56 | tf_op jit(solution)/shard_map/ppermute | solution.py:47
  69.6 9.0 %collective-permute-start.12 = (f32[4,128,128]{2,1,0:T(8,128)S(1)}, f32[4,128,128]{2,1,0:T(8,128)S(1)}, u32[]{:S(2)}, u32[]{:S(2)}) collective-permute-start(f32[4,128,128]{2,1,0:T(8,128)S(1)} %select_add_fusion.1), channel_id=1, source_target_pairs={{0,128},{64,192},{128,0},{192,64},{1,129},{65,193},{129,1},{193,65... | collective-permute-start | bytes 786440 | tf_op jit(solution)/shard_map/ppermute | solution.py:47
  72.4 12.6 %collective-permute-start.11 = (f32[4,128,128]{2,1,0:T(8,128)S(1)}, f32[4,128,128]{2,1,0:T(8,128)S(1)}, u32[]{:S(2)}, u32[]{:S(2)}) collective-permute-start(f32[4,128,128]{2,1,0:T(8,128)S(1)} %select_add_fusion.1), channel_id=1, source_target_pairs={{0,64},{64,128},{128,192},{192,0},{1,65},{65,129},{129,193},{193,1... | collective-permute-start | bytes 786440 | tf_op jit(solution)/shard_map/ppermute | solution.py:47
  72.8 12.3 %collective-permute-start.13 = (f32[4,128,128]{2,1,0:T(8,128)S(1)}, f32[4,128,128]{2,1,0:T(8,128)S(1)}, u32[]{:S(2)}, u32[]{:S(2)}) collective-permute-start(f32[4,128,128]{2,1,0:T(8,128)S(1)} %select_add_fusion.1), channel_id=1, source_target_pairs={{0,192},{64,0},{128,64},{192,128},{1,193},{65,1},{129,65},{193,129... | collective-permute-start | bytes 786440 | tf_op jit(solution)/shard_map/ppermute | solution.py:47
  86.5 3.6 %collective-permute-start.14 = (f32[4,128,128]{2,1,0:T(8,128)}, f32[4,128,128]{2,1,0:T(8,128)}, u32[]{:S(2)}, u32[]{:S(2)}) collective-permute-start(f32[4,128,128]{2,1,0:T(8,128)} %select_add_fusion), channel_id=1, source_target_pairs={{0,8},{8,0},{1,9},{9,1},{2,10},{10,2},{3,11},{11,3},{4,12},{12,4},... | collective-permute-start | bytes 786440 | tf_op jit(solution)/shard_map/ppermute | solution.py:40
  93.1 56.7 %copy-start.4 = (s32[256,2]{0,1:T(2,128)S(1)}, s32[256,2]{0,1:T(2,128)}, u32[]{:S(2)}) copy-start(s32[256,2]{0,1:T(2,128)} %param.15) | copy-start | bytes 6148
  93.1 92.3 %reduce-scatter.2.cloned.1.call-start = ((), (), s32[]{:S(2)}) async-start(), calls=%async_computation.3 | async-start | bytes 1769472 | tf_op jit(solution)/shard_map/reduce_scatter | solution.py:129
  149.8 134.0 %all-gather.5.cloned.1.call-start = ((), (), s32[]{:S(2)}) async-start(), calls=%async_computation.4 | async-start | bytes 12976128 | tf_op jit(solution)/shard_map/all_gather | solution.py:156
  290.9 8.2 %copy-start.1 = (bf16[1024,6144]{0,1:T(8,128)(2,1)S(1)}, bf16[1024,6144]{0,1:T(8,128)(2,1)}, u32[]{:S(2)}) copy-start(bf16[1024,6144]{0,1:T(8,128)(2,1)} %all-gather.5.cloned.1.call-done) | copy-start | bytes 37748740
  290.9 9.2 %copy-start.5 = (bf16[1,288,6144]{2,1,0:T(8,128)(2,1)S(1)}, bf16[1,288,6144]{2,1,0:T(8,128)(2,1)}, u32[]{:S(2)}) copy-start(bf16[1,288,6144]{2,1,0:T(8,128)(2,1)} %param.17) | copy-start | bytes 10616836
Sparse Core Ops, SparseCore 0:
  93.2 51.5 all-gather.2
  149.9 35.4 reduce-scatter.1
  214.6 69.1 all-gather.4
where the time goes:
time: 313 us; the launch traced here: 311 us
  waiting for transfers between devices  163 us (52%)
  between operations  33.7 us (11%)
  other arithmetic  28.5 us (9%)
  local copies, waits for them, and re-layouts  27.5 us (9%)
  matrix products  23.6 us (8%)
  starting transfers between devices  19.1 us (6%)
  blocking collectives  15.8 us (5%)
    all_gather x1, waiting for transfers between devices, body(): row_block = lax.all_gather(slices, SEQ, axis=1, tiled=True)  69.3 us
    all_gather x1, waiting for transfers between devices, body(): gathered = lax.all_gather(normed, SEQ, axis=0, tiled=True)  51.6 us
    reduce_scatter x1, waiting for transfers between devices, body(): lax.psum_scatter(jnp.dot(row_block, out_weight, preferred_element_type=jn...  22.7 us
    ppermute x12, waiting for transfers between devices, prefix_over(): lax.ppermute(part, axis, [(i, (i + d) % peers) for i in range(peers)])  19.6 us
    all_to_all x1, blocking collectives, body(): lax.all_to_all(buffer.reshape(experts, capacity, columns), 'exp', split_a...  15.8 us
    ppermute x12, starting transfers between devices, prefix_over(): lax.ppermute(part, axis, [(i, (i + d) % peers) for i in range(peers)])  15.2 us
    dot_general x1, other arithmetic, body(): jnp.einsum('rd,rd->r', row_block, row_block, preferred_element_type=jnp.f...  7.08 us
    dot_general x1, matrix products, body(): lax.dot_general(w_gate, row_block, contract_last, preferred_element_type=...  6.96 us
  transfers between devices with their start and end apart: 18, of which 8 were waited for; matrix products, arithmetic and copies ran while one was open for 10% of the time, Pallas kernels for 0%

commit v1 on v0

--- a/solution.py
+++ b/solution.py
@@ -3,6 +3,7 @@
 from jax import lax
 from jax.sharding import Mesh
 from jax.sharding import PartitionSpec as P
+from jax.lax import all_to_all, axis_size
 
 D = 6144
 HEAD_DIM = 128
@@ -101,6 +102,12 @@
     gate_weight,
     up_weight,
 ):
+
+    def guide_roots_here(axis_id, local_x):
+        t1 = jnp.stack([local_x for _ in range(axis_size(axis_id))])
+        out_arr = all_to_all(t1, axis_id, 0, 0)
+        return jnp.concatenate(out_arr, 1)
+
     positions, head_cols = query_rows.shape
     heads_here = head_cols // HEAD_DIM
     queries = query_rows.astype(jnp.float32).reshape(positions, heads_here, HEAD_DIM)
@@ -153,7 +160,7 @@
     )
     sources, entries, gathered_columns = received.shape
     slices = received.reshape(sources * entries, gathered_columns)
-    row_block = lax.all_gather(slices, SEQ, axis=1, tiled=True)
+    row_block = guide_roots_here(SEQ, slices)
     squares = jnp.einsum("rd,rd->r", row_block, row_block, preferred_element_type=jnp.float32)
     gate_sum = lax.dot_general(w_gate, row_block, contract_last, preferred_element_type=jnp.float32)
     up_sum = lax.dot_general(w_up, row_block, contract_last, preferred_element_type=jnp.float32)

time: 313 us -> 402 us (1.28)
  blocking collectives: 15.8 us -> 168 us
  waiting for transfers between devices: 163 us -> 93.9 us
  local copies, waits for them, and re-layouts: 27.5 us -> 33 us
    all_to_all x0 -> x1, blocking collectives: none -> 153 us  [guide_roots_here(): out_arr = all_to_all(t1, axis_id, 0, 0)]
    all_gather x1 -> x0, waiting for transfers between devices: 69.3 us -> none  [body(): row_block = lax.all_gather(slices, SEQ, axis=1, tiled=True)]
    another operation x1 -> x3, local copies, waits for them, and re-layouts: 0.69 us -> 6.92 us  [the longest x2 6.24 us: guide_roots_here(): t1 = jnp.stack([local_x for _ in range(axis_size(axis_id))])]
  transfers between devices with their start and end apart: 18 -> 17, of which waited for: 8 -> 7; matrix products, arithmetic and copies ran while one was open for 10% -> 8% of each run, Pallas kernels for 0% -> 0%
where the time goes in v1:
time: 402 us; the launch traced here: 400 us
  blocking collectives  168 us (42%)
  waiting for transfers between devices  93.9 us (23%)
  between operations  34 us (8%)
  local copies, waits for them, and re-layouts  33 us (8%)
  other arithmetic  28.5 us (7%)
  matrix products  23.6 us (6%)
  starting transfers between devices  19.1 us (5%)
    all_to_all x1, blocking collectives, guide_roots_here(): out_arr = all_to_all(t1, axis_id, 0, 0)  153 us
    all_gather x1, waiting for transfers between devices, body(): gathered = lax.all_gather(normed, SEQ, axis=0, tiled=True)  51.6 us
    reduce_scatter x1, waiting for transfers between devices, body(): lax.psum_scatter(jnp.dot(row_block, out_weight, preferred_element_type=jn...  22.7 us
    ppermute x12, waiting for transfers between devices, prefix_over(): lax.ppermute(part, axis, [(i, (i + d) % peers) for i in range(peers)])  19.6 us
    all_to_all x1, blocking collectives, body(): lax.all_to_all(buffer.reshape(experts, capacity, columns), 'exp', split_a...  15.8 us
    ppermute x12, starting transfers between devices, prefix_over(): lax.ppermute(part, axis, [(i, (i + d) % peers) for i in range(peers)])  15.2 us
  transfers between devices with their start and end apart: 17, of which 7 were waited for; matrix products, arithmetic and copies ran while one was open for 8% of the time, Pallas kernels for 0%

profile of v1, /device:TPU:1, one launch (start us, length us, event | category | flops | bytes accessed | tf_op | source)
XLA Modules:
  0.0 400.5 jit_solution(4496793939262456295)
XLA Ops:
  7.2 1.5 copy.69
  8.8 1.4 reduce_window_sum.26
  10.9 3.2 collective-permute-start
  17.0 2.4 fusion.36
  49.0 2.3 collective-permute-start.3
  55.4 2.5 collective-permute-start.6
  58.5 1.9 collective-permute-done.10
  62.0 7.3 %collective-permute-done.8 = f32[4,128,128]{2,1,0:T(8,128)S(1)} collective-permute-done((f32[4,128,128]{2,1,0:T(8,128)S(1)}, f32[4,128,128]{2,1,0:T(8,128)S(1)}, u32[]{:S(2)}, u32[]{:S(2)}) %collective-permute-start.8) | collective-permute-done | bytes 262176 | tf_op jit(solution)/shard_map/ppermute | solution.py:48
  69.6 2.8 collective-permute-start.12
  72.8 2.4 collective-permute-start.13
  75.2 3.5 collective-permute-done.12
  78.6 6.4 %collective-permute-done.11 = f32[4,128,128]{2,1,0:T(8,128)S(1)} collective-permute-done((f32[4,128,128]{2,1,0:T(8,128)S(1)}, f32[4,128,128]{2,1,0:T(8,128)S(1)}, u32[]{:S(2)}, u32[]{:S(2)}) %collective-permute-start.11) | collective-permute-done | bytes 262176 | tf_op jit(solution)/shard_map/ppermute | solution.py:48
  85.0 1.4 select_add_fusion
  90.1 2.2 multiply_reduce_fusion
  93.2 51.6 %all-gather.2.cloned.1.call-done = bf16[2048,1024]{1,0:T(8,128)(2,1)} async-done(((bf16[64,1024]{1,0:T(8,128)(2,1)}), bf16[2048,1024]{1,0:T(8,128)(2,1)}) %all-gather.2.cloned.1.call-update) | async-done | bytes 4194320 | tf_op jit(solution)/shard_map/all_gather | solution.py:134
  144.8 5.0 %fusion.62 = f32[2048,192]{0,1:T(8,128)} fusion(bf16[2048,1024]{1,0:T(8,128)(2,1)} %all-gather.2.cloned.1.call-done, bf16[1024,192]{0,1:T(8,128)(2,1)} %param.13), kind=kOutput, calls=%fused_computation.128 | convolution fusion | flops 805306368 | bytes 6160384 | tf_op jit(solution)/shard_map/dot_general | solution.py:137
  151.7 1.6 eq.212
  154.1 1.6 mul.219
  156.3 2.2 reduce-window.6
  162.7 22.7 %reduce-scatter.2.cloned.1.call-done = f32[256,192]{0,1:T(8,128)} async-done(((f32[2048,192]{0,1:T(8,128)}), f32[256,192]{0,1:T(8,128)}) %reduce-scatter.2.cloned.1.call-update) | async-done | bytes 196624 | tf_op jit(solution)/shard_map/reduce_scatter | solution.py:136
  185.4 1.6 add_convert_fusion
  187.1 1.6 copy.84
  188.7 1.7 broadcast_in_dim.122
  190.5 1.9 reshape.151
  192.3 3.5 scatter_custom_fusion
  195.9 2.0 copy.85
  197.9 15.8 %all_to_all.10 = bf16[8,128,192]{1,2,0:T(8,128)(2,1)S(1)} all-to-all(bf16[8,128,192]{1,2,0:T(8,128)(2,1)} %copy.85), channel_id=1, replica_groups=mesh['seq_0'=4,'seq_1'=4,'seq_2'=2,'exp'=8] {'exp'}, dimensions={0} | all-to-all | bytes 786432 | tf_op jit(solution)/shard_map/all_to_all | solution.py:158
  213.7 6.2 %stack.203 = bf16[32,1024,192]{1,2,0:T(8,128)(2,1)} broadcast(bf16[1024,192]{0,1:T(8,128)(2,1)S(1)} %copy_bitcast_fusion), dimensions={1,2} | broadcast | bytes 12976128 | tf_op jit(solution)/shard_map/stack | solution.py:107
  219.9 152.6 %all_to_all.11 = bf16[32,1024,192]{1,2,0:T(8,128)(2,1)} all-to-all(bf16[32,1024,192]{1,2,0:T(8,128)(2,1)} %stack.203), channel_id=1, replica_groups=mesh['seq_0'=4,'seq_1'=4,'seq_2'=2,'exp'=8] {'seq_0','seq_1','seq_2'}, dimensions={0} | all-to-all | bytes 25165824 | tf_op jit(solution)/shard_map/all_to_all | solution.py:108
  372.4 7.1 %fusion = f32[1024]{0:T(1024)S(1)} fusion(bf16[32,1024,192]{1,2,0:T(8,128)(2,1)} %all_to_all.11), kind=kLoop, calls=%fused_computation.2 | loop fusion | flops 18873344 | bytes 12587008 | tf_op jit(solution)/shard_map/rd,rd->r/dot_general | solution.py:164
  379.6 7.0 %fusion.17 = f32[288,1024]{1,0:T(8,128)S(1)} fusion(bf16[1024,6144]{0,1:T(8,128)(2,1)} %bitcast.152, bf16[1,288,6144]{2,1,0:T(8,128)(2,1)S(1)} %copy-done, f32[1024]{0:T(1024)S(1)} %add_rsqrt_fusion), kind=kOutput, calls=%fused_computation.11 | convolution fusion | flops 3624173568 | bytes 17305600 | tf_op jit(solution)/shard_map/dot_general | solution.py:165
  388.7 4.9 %fusion.23 = bf16[1,288,1024]{2,1,0:T(8,128)(2,1)} fusion(bf16[1024,6144]{0,1:T(8,128)(2,1)S(1)} %bitcast.153, bf16[1,288,6144]{2,1,0:T(8,128)(2,1)S(1)} %copy-done.5, f32[288,1024]{1,0:T(8,128)S(1)} %fusion.17, f32[1024]{0:T(1024)S(1)} %add_rsqrt_fusion), kind=kOutput, calls=%fused_computation.13 | convolution fusion | flops 3625943040 | bytes 17895424 | tf_op jit(solution)/shard_map/dot_general | solution.py:166
  (89 shorter events, 34.5 us)
Async XLA Ops:
  7.2 372.4 %copy-start = (bf16[1,288,6144]{2,1,0:T(8,128)(2,1)S(1)}, bf16[1,288,6144]{2,1,0:T(8,128)(2,1)}, u32[]{:S(2)}) copy-start(bf16[1,288,6144]{2,1,0:T(8,128)(2,1)} %param.16) | copy-start | bytes 10616836
  7.2 137.6 %all-gather.2.cloned.1.call-start = ((), (), s32[]{:S(2)}) async-start(), calls=%async_computation.3 | async-start | bytes 4325376 | tf_op jit(solution)/shard_map/all_gather | solution.py:134
  10.9 35.7 %collective-permute-start = (f32[8]{0:T(128)S(1)}, f32[8]{0:T(128)S(1)}, u32[]{:S(2)}, u32[]{:S(2)}) collective-permute-start(f32[8]{0:T(128)S(1)} %fusion.59), channel_id=1, source_target_pairs={{0,8},{8,0},{1,9},{9,1},{2,10},{10,2},{3,11},{11,3},{4,12},{12,4},... | collective-permute-start | bytes 104 | tf_op jit(solution)/shard_map/ppermute | solution.py:41
  19.5 31.9 %collective-permute-start.7 = (f32[8,128,128]{2,1,0:T(8,128)}, f32[8,128,128]{2,1,0:T(8,128)}, u32[]{:S(2)}, u32[]{:S(2)}) collective-permute-start(f32[8,128,128]{2,1,0:T(8,128)} %fusion.36), channel_id=1, source_target_pairs={{0,8},{8,0},{1,9},{9,1},{2,10},{10,2},{3,11},{11,3},{4,12},{12,4},... | collective-permute-start | bytes 1572872 | tf_op jit(solution)/shard_map/ppermute | solution.py:41
  46.6 40.5 %copy-start.3 = (bf16[64,1024]{1,0:T(8,128)(2,1)S(1)}, bf16[64,1024]{1,0:T(8,128)(2,1)}, u32[]{:S(2)}) copy-start(bf16[64,1024]{1,0:T(8,128)(2,1)} %param.10) | copy-start | bytes 393220
  46.6 40.5 %copy-start.6 = (bf16[64,1024]{1,0:T(8,128)(2,1)S(1)}, bf16[64,1024]{1,0:T(8,128)(2,1)}, u32[]{:S(2)}) copy-start(bf16[64,1024]{1,0:T(8,128)(2,1)} %param.9) | copy-start | bytes 393220
  47.4 7.4 %collective-permute-start.2 = (f32[4]{0:T(128)S(1)}, f32[4]{0:T(128)S(1)}, u32[]{:S(2)}, u32[]{:S(2)}) collective-permute-start(f32[4]{0:T(128)S(1)} %dynamic_slice.6), channel_id=1, source_target_pairs={{0,32},{16,48},{32,0},{48,16},{1,33},{17,49},{33,1},{49,17},{2,34}... | collective-permute-start | bytes 56 | tf_op jit(solution)/shard_map/ppermute | solution.py:48
  48.6 6.7 %collective-permute-start.1 = (f32[4]{0:T(128)S(1)}, f32[4]{0:T(128)S(1)}, u32[]{:S(2)}, u32[]{:S(2)}) collective-permute-start(f32[4]{0:T(128)S(1)} %dynamic_slice.6), channel_id=1, source_target_pairs={{0,16},{16,32},{32,48},{48,0},{1,17},{17,33},{33,49},{49,1},{2,18}... | collective-permute-start | bytes 56 | tf_op jit(solution)/shard_map/ppermute | solution.py:48
  49.0 6.3 %collective-permute-start.3 = (f32[4]{0:T(128)S(1)}, f32[4]{0:T(128)S(1)}, u32[]{:S(2)}, u32[]{:S(2)}) collective-permute-start(f32[4]{0:T(128)S(1)} %dynamic_slice.6), channel_id=1, source_target_pairs={{0,48},{16,0},{32,16},{48,32},{1,49},{17,1},{33,17},{49,33},{2,50}... | collective-permute-start | bytes 56 | tf_op jit(solution)/shard_map/ppermute | solution.py:48
  52.5 16.9 %copy-start.2 = (f32[8,128,128]{2,1,0:T(8,128)}, f32[8,128,128]{2,1,0:T(8,128)S(1)}, u32[]{:S(2)}) copy-start(f32[8,128,128]{2,1,0:T(8,128)S(1)} %broadcast_select_fusion) | copy-start | bytes 1572868
  53.8 6.5 %collective-permute-start.10 = (f32[4,128,128]{2,1,0:T(8,128)S(1)}, f32[4,128,128]{2,1,0:T(8,128)S(1)}, u32[]{:S(2)}, u32[]{:S(2)}) collective-permute-start(f32[4,128,128]{2,1,0:T(8,128)S(1)} %fusion.30), channel_id=1, source_target_pairs={{0,48},{16,0},{32,16},{48,32},{1,49},{17,1},{33,17},{49,33},{2,50}... | collective-permute-start | bytes 786440 | tf_op jit(solution)/shard_map/ppermute | solution.py:48
  53.9 8.1 %collective-permute-start.9 = (f32[4,128,128]{2,1,0:T(8,128)S(1)}, f32[4,128,128]{2,1,0:T(8,128)S(1)}, u32[]{:S(2)}, u32[]{:S(2)}) collective-permute-start(f32[4,128,128]{2,1,0:T(8,128)S(1)} %fusion.30), channel_id=1, source_target_pairs={{0,32},{16,48},{32,0},{48,16},{1,33},{17,49},{33,1},{49,17},{2,34}... | collective-permute-start | bytes 786440 | tf_op jit(solution)/shard_map/ppermute | solution.py:48
  54.9 14.5 %collective-permute-start.8 = (f32[4,128,128]{2,1,0:T(8,128)S(1)}, f32[4,128,128]{2,1,0:T(8,128)S(1)}, u32[]{:S(2)}, u32[]{:S(2)}) collective-permute-start(f32[4,128,128]{2,1,0:T(8,128)S(1)} %fusion.30), channel_id=1, source_target_pairs={{0,16},{16,32},{32,48},{48,0},{1,17},{17,33},{33,49},{49,1},{2,18}... | collective-permute-start | bytes 786440 | tf_op jit(solution)/shard_map/ppermute | solution.py:48
  55.4 17.3 %collective-permute-start.6 = (f32[4]{0:T(128)S(1)}, f32[4]{0:T(128)S(1)}, u32[]{:S(2)}, u32[]{:S(2)}) collective-permute-start(f32[4]{0:T(128)S(1)} %get-tuple-element.19), channel_id=1, source_target_pairs={{0,192},{64,0},{128,64},{192,128},{1,193},{65,1},{129,65},{193,129... | collective-permute-start | bytes 56 | tf_op jit(solution)/shard_map/ppermute | solution.py:48
  57.9 17.2 %collective-permute-start.5 = (f32[4]{0:T(128)S(1)}, f32[4]{0:T(128)S(1)}, u32[]{:S(2)}, u32[]{:S(2)}) collective-permute-start(f32[4]{0:T(128)S(1)} %get-tuple-element.19), channel_id=1, source_target_pairs={{0,128},{64,192},{128,0},{192,64},{1,129},{65,193},{129,1},{193,65... | collective-permute-start | bytes 56 | tf_op jit(solution)/shard_map/ppermute | solution.py:48
  60.3 14.8 %collective-permute-start.4 = (f32[4]{0:T(128)S(1)}, f32[4]{0:T(128)S(1)}, u32[]{:S(2)}, u32[]{:S(2)}) collective-permute-start(f32[4]{0:T(128)S(1)} %get-tuple-element.19), channel_id=1, source_target_pairs={{0,64},{64,128},{128,192},{192,0},{1,65},{65,129},{129,193},{193,1... | collective-permute-start | bytes 56 | tf_op jit(solution)/shard_map/ppermute | solution.py:48
  69.6 9.0 %collective-permute-start.12 = (f32[4,128,128]{2,1,0:T(8,128)S(1)}, f32[4,128,128]{2,1,0:T(8,128)S(1)}, u32[]{:S(2)}, u32[]{:S(2)}) collective-permute-start(f32[4,128,128]{2,1,0:T(8,128)S(1)} %select_add_fusion.1), channel_id=1, source_target_pairs={{0,128},{64,192},{128,0},{192,64},{1,129},{65,193},{129,1},{193,65... | collective-permute-start | bytes 786440 | tf_op jit(solution)/shard_map/ppermute | solution.py:48
  72.4 12.6 %collective-permute-start.11 = (f32[4,128,128]{2,1,0:T(8,128)S(1)}, f32[4,128,128]{2,1,0:T(8,128)S(1)}, u32[]{:S(2)}, u32[]{:S(2)}) collective-permute-start(f32[4,128,128]{2,1,0:T(8,128)S(1)} %select_add_fusion.1), channel_id=1, source_target_pairs={{0,64},{64,128},{128,192},{192,0},{1,65},{65,129},{129,193},{193,1... | collective-permute-start | bytes 786440 | tf_op jit(solution)/shard_map/ppermute | solution.py:48
  72.8 12.3 %collective-permute-start.13 = (f32[4,128,128]{2,1,0:T(8,128)S(1)}, f32[4,128,128]{2,1,0:T(8,128)S(1)}, u32[]{:S(2)}, u32[]{:S(2)}) collective-permute-start(f32[4,128,128]{2,1,0:T(8,128)S(1)} %select_add_fusion.1), channel_id=1, source_target_pairs={{0,192},{64,0},{128,64},{192,128},{1,193},{65,1},{129,65},{193,129... | collective-permute-start | bytes 786440 | tf_op jit(solution)/shard_map/ppermute | solution.py:48
  86.5 3.6 collective-permute-start.14
  93.1 56.7 %copy-start.4 = (s32[256,2]{0,1:T(2,128)S(1)}, s32[256,2]{0,1:T(2,128)}, u32[]{:S(2)}) copy-start(s32[256,2]{0,1:T(2,128)} %param.15) | copy-start | bytes 6148
  93.1 92.3 %reduce-scatter.2.cloned.1.call-start = ((), (), s32[]{:S(2)}) async-start(), calls=%async_computation.4 | async-start | bytes 1769472 | tf_op jit(solution)/shard_map/reduce_scatter | solution.py:136
  379.5 8.2 %copy-start.1 = (bf16[32,1024,192]{1,2,0:T(8,128)(2,1)S(1)}, bf16[32,1024,192]{1,2,0:T(8,128)(2,1)}, u32[]{:S(2)}) copy-start(bf16[32,1024,192]{1,2,0:T(8,128)(2,1)} %all_to_all.11) | copy-start | bytes 37748740
  379.6 9.2 %copy-start.5 = (bf16[1,288,6144]{2,1,0:T(8,128)(2,1)S(1)}, bf16[1,288,6144]{2,1,0:T(8,128)(2,1)}, u32[]{:S(2)}) copy-start(bf16[1,288,6144]{2,1,0:T(8,128)(2,1)} %param.17) | copy-start | bytes 10616836
Sparse Core Ops, SparseCore 0:
  93.2 51.5 all-gather.1
  149.9 35.4 reduce-scatter.1
